TPU v7x, 256 devices: a whole 4x4x8 slice. The times are simulated.
256 devices in a mesh: dp: 32 (over z, y), tensor: 8 (over x, core).
Axes of the slice: x: 4, y: 4, z: 8, core: 2. Of those that a mesh axis runs over, the one named last changes fastest.
Arguments:
- tokens: bfloat16 [4096, 4096], P('dp', 'tensor'), may hold values from -6 to 6
- grad_out: bfloat16 [4096, 4096], P('dp', 'tensor'), may hold values from -6 to 6
- gate_blocks: int32 [8, 32], P('tensor'), may hold values from -1 to 447, as said below
- gate_values: bfloat16 [8, 32, 128, 128], P('tensor'), may hold values from -0.375 to 0.375
- up_blocks: int32 [8, 32], P('tensor'), may hold values from -1 to 447, as said below
- up_values: bfloat16 [8, 32, 128, 128], P('tensor'), may hold values from -0.375 to 0.375
- down_blocks: int32 [8, 32], P('tensor'), may hold values from -1 to 447, as said below
- down_values: bfloat16 [8, 32, 128, 128], P('tensor'), may hold values from -0.1875 to 0.1875
Outputs:
- mixed: bfloat16 [4096, 4096], P('dp', 'tensor')
- grad_tokens: bfloat16 [4096, 4096], P('dp', 'tensor')
- grad_gate: float32 [8, 32, 128, 128], P('tensor', 'dp')
- grad_up: float32 [8, 32, 128, 128], P('tensor', 'dp')
- grad_down: float32 [8, 32, 128, 128], P('tensor', 'dp')
Inputs may be any that keep to these rules, and one draw needn't show every extreme that they name: `gate_blocks`: each row lists distinct block numbers of one tensor shard in its first slots and -1 in the rest; a row has 16 to 32 listed blocks, one row has exactly 32 and another exactly 16. `up_blocks`: as for gate_blocks, drawn apart. `down_blocks`: as for gate_blocks, drawn apart.
All inputs are finite; a program needn't handle non-finite values.
Results may differ from a plain program's by a relative error of at most 0.015.
Values may be sent and summed in bfloat16 or wider, within the bound.
No kernel may reach another device: no remote copies, remote signals or barrier semaphores. Data moves between devices by JAX's collectives and lax.ppermute only.
A program may use at most 64 MiB of HBM per device.

v0:
```python
import jax
import jax.numpy as jnp
from jax import lax
from jax.sharding import PartitionSpec as P

FF = 14336


def locate(blocks, feature_count):
    flat = blocks[0]
    weight = (flat >= 0).astype(jnp.float32)
    safe = jnp.maximum(flat, 0)
    return (safe // feature_count, safe % feature_count, weight)


def one_hot(targets, weight, count):
    return (targets[:, None] == jnp.arange(count)[None, :]).astype(jnp.float32) * weight[:, None]


def spread(product, table):
    return jnp.einsum("tsn,sc->tcn", product, table, precision=lax.Precision.HIGHEST)


def select(source, position):
    return jnp.take(source, position, axis=1)


def forward_blocks(rows_in, values):
    return jnp.einsum("tsk,skn->tsn", rows_in, values, preferred_element_type=jnp.float32)


def backward_blocks(rows_in, values):
    return jnp.einsum("tsn,skn->tsk", rows_in, values, preferred_element_type=jnp.float32)


def slot_term(left, right, weight):
    product = jnp.einsum("tsk,tsn->skn", left, right, preferred_element_type=jnp.float32)
    return product * weight[:, None, None]


def body(
    tokens, grad_out, gate_blocks, gate_values, up_blocks, up_values, down_blocks, down_values
):
    gathered_x, gathered_dy = (
        lax.all_gather(tokens, "tensor", axis=1, tiled=True),
        lax.all_gather(grad_out, "tensor", axis=1, tiled=True),
    )
    tok_rows, feature_width = gathered_x.shape
    block_size = gate_values.shape[-1]
    feature_count = feature_width // block_size
    hidden_count = FF // (block_size * lax.axis_size("tensor"))
    inputs = gathered_x.reshape(tok_rows, feature_count, block_size)
    upstream = gathered_dy.reshape(tok_rows, feature_count, block_size)
    gate_hid, gate_feat, gate_live = locate(gate_blocks, feature_count)
    up_hid, up_feat, up_live = locate(up_blocks, feature_count)
    down_hid, down_feat, down_live = locate(down_blocks, feature_count)
    gate_rows = select(inputs, gate_feat)
    up_rows = select(inputs, up_feat)
    gate_pre = spread(
        forward_blocks(gate_rows, gate_values[0]), one_hot(gate_hid, gate_live, hidden_count)
    )
    up_pre = spread(forward_blocks(up_rows, up_values[0]), one_hot(up_hid, up_live, hidden_count))
    sigma_gate = jax.nn.sigmoid(gate_pre)
    activated = gate_pre * sigma_gate
    hidden = (activated * up_pre).astype(jnp.bfloat16)
    hidden_rows = select(hidden, down_hid)
    mixed_part = spread(
        forward_blocks(hidden_rows, down_values[0]), one_hot(down_feat, down_live, feature_count)
    )
    mixed_part = mixed_part.reshape(tok_rows, feature_width)
    upstream_rows = select(upstream, down_feat)
    mixed = lax.psum_scatter(
        mixed_part.astype(jnp.bfloat16), "tensor", scatter_dimension=1, tiled=True
    )
    hidden_grad = spread(
        backward_blocks(upstream_rows, down_values[0]), one_hot(down_hid, down_live, hidden_count)
    )
    gate_delta = (hidden_grad * up_pre * sigma_gate * (1.0 + gate_pre * (1.0 - sigma_gate))).astype(
        jnp.bfloat16
    )
    up_delta = (hidden_grad * activated).astype(jnp.bfloat16)
    gate_delta_rows = select(gate_delta, gate_hid)
    up_delta_rows = select(up_delta, up_hid)
    input_part = spread(
        backward_blocks(gate_delta_rows, gate_values[0]),
        one_hot(gate_feat, gate_live, feature_count),
    )
    input_part = input_part + spread(
        backward_blocks(up_delta_rows, up_values[0]), one_hot(up_feat, up_live, feature_count)
    )
    input_part = input_part.reshape(tok_rows, feature_width)
    gate_term = slot_term(gate_rows, gate_delta_rows, gate_live)
    up_term = slot_term(up_rows, up_delta_rows, up_live)
    down_term = slot_term(hidden_rows, upstream_rows, down_live)
    grad_gate, grad_up, grad_down = (
        lax.psum_scatter(term.astype(jnp.bfloat16), "dp", scatter_dimension=0, tiled=True).astype(
            jnp.float32
        )[None]
        for term in (gate_term, up_term, down_term)
    )
    grad_tokens = lax.psum_scatter(
        input_part.astype(jnp.bfloat16), "tensor", scatter_dimension=1, tiled=True
    )
    return (mixed, grad_tokens, grad_gate, grad_up, grad_down)


def solution(mesh):
    in_specs = (
        P("dp", "tensor"),
        P("dp", "tensor"),
        P("tensor", None),
        P("tensor", None, None, None),
        P("tensor", None),
        P("tensor", None, None, None),
        P("tensor", None),
        P("tensor", None, None, None),
    )
    out_specs = (
        P("dp", "tensor"),
        P("dp", "tensor"),
        P("tensor", "dp", None, None),
        P("tensor", "dp", None, None),
        P("tensor", "dp", None, None),
    )
    return jax.shard_map(body, mesh=mesh, in_specs=in_specs, out_specs=out_specs, check_vma=False)
```

profile of v0, /device:TPU:8, one launch (start us, length us, event | category | flops | bytes accessed | tf_op | source)
XLA Modules:
  0.0 825.7 jit_solution(16852433310537458351)
XLA Ops:
  7.2 0.0 copy-start
  7.2 0.0 all-gather.3.cloned.1.call-start
  7.2 1.7 copy.39
  9.0 0.0 all-gather.3.cloned.1.call-update
  9.0 0.0 all-gather.5.cloned.1.call-start
  9.0 1.7 copy.47
  10.7 0.0 all-gather.5.cloned.1.call-update
  10.7 0.0 reduce-scatter.10.cloned.1.call-start
  10.8 0.7 compare_and_fusion
  11.5 0.7 compare_and_fusion.2
  12.2 0.7 compare_and_fusion.1
  12.9 0.7 fusion.78
  13.6 0.7 fusion.79
  14.2 0.7 fusion.77
  14.9 24.2 %all-gather.3.cloned.1.call-done = bf16[128,4096]{0,1:T(8,128)(2,1)} async-done(((bf16[128,512]{0,1:T(8,128)(2,1)}), bf16[128,4096]{0,1:T(8,128)(2,1)}) %all-gather.3.cloned.1.call-update) | async-done | bytes 1048592 | tf_op jit(solution)/shard_map/all_gather | solution.py:45
  39.1 1.6 copy.40
  40.7 26.5 %all-gather.5.cloned.1.call-done = bf16[128,4096]{0,1:T(8,128)(2,1)} async-done(((bf16[128,512]{0,1:T(8,128)(2,1)}), bf16[128,4096]{0,1:T(8,128)(2,1)}) %all-gather.5.cloned.1.call-update) | async-done | bytes 1048592 | tf_op jit(solution)/shard_map/all_gather | solution.py:46
  67.2 2.3 copy.48
  69.5 1.7 gather_fusion.1
  71.2 1.7 gather_fusion
  72.8 3.0 gather_fusion.3
  75.8 0.0 copy-done.2
  75.8 0.0 copy-done.8
  75.8 0.5 convolution_bitcast_fusion.5
  76.3 0.0 copy-start.1
  76.3 2.2 fusion.10
  78.6 0.5 convolution_bitcast_fusion.4
  79.1 2.2 fusion.8
  81.4 0.9 convolution_bitcast_fusion.2
  82.3 2.2 fusion.4
  84.5 1.1 fusion.37
  85.6 1.7 gather_fusion.4
  87.2 3.2 multiply_convert_fusion.2
  90.4 0.0 reduce-scatter.10.cloned.1.call-update
  90.5 0.2 reduce-scatter.14.cloned.1.call-start
  90.7 1.7 gather_fusion.2
  92.4 3.2 multiply_convert_fusion
  95.6 0.0 reduce-scatter.14.cloned.1.call-update
  95.6 0.0 reduce-scatter.12.cloned.1.call-start
  95.7 1.6 gather_fusion.5
  97.3 3.3 multiply_convert_fusion.1
  100.6 0.0 reduce-scatter.12.cloned.1.call-update
  100.6 0.0 reduce-scatter.6.cloned.1.call-start
  100.7 0.5 convolution_bitcast_fusion.3
  101.2 3.0 fusion.14
  104.2 1.4 copy.90
  105.6 0.0 reduce-scatter.6.cloned.1.call-update
  105.6 0.0 copy-start.3
  105.6 0.0 reduce-scatter.8.cloned.1.call-start
  105.7 2.3 convolution_bitcast_fusion
  108.0 0.0 copy-done.4
  108.0 0.9 convolution_bitcast_fusion.1
  108.9 3.0 fusion
  111.9 3.1 add_convert_fusion
  115.0 1.4 copy.89
  116.4 0.0 reduce-scatter.8.cloned.1.call-update
  116.5 190.5 %reduce-scatter.10.cloned.1.call-done = bf16[1,128,128]{2,1,0:T(8,128)(2,1)} async-done(((bf16[32,128,128]{2,1,0:T(8,128)(2,1)}), bf16[1,128,128]{2,1,0:T(8,128)(2,1)}) %reduce-scatter.10.cloned.1.call-update) | async-done | bytes 32784 | tf_op jit(solution)/shard_map/reduce_scatter | solution.py:96
  307.0 1.4 bitcast_convert_fusion.2
  308.4 217.8 %reduce-scatter.14.cloned.1.call-done = bf16[1,128,128]{2,1,0:T(8,128)(2,1)} async-done(((bf16[32,128,128]{2,1,0:T(8,128)(2,1)}), bf16[1,128,128]{2,1,0:T(8,128)(2,1)}) %reduce-scatter.14.cloned.1.call-update) | async-done | bytes 32784 | tf_op jit(solution)/shard_map/reduce_scatter | solution.py:96
  526.2 1.4 bitcast_convert_fusion
  527.6 217.8 %reduce-scatter.12.cloned.1.call-done = bf16[1,128,128]{2,1,0:T(8,128)(2,1)} async-done(((bf16[32,128,128]{2,1,0:T(8,128)(2,1)}), bf16[1,128,128]{2,1,0:T(8,128)(2,1)}) %reduce-scatter.12.cloned.1.call-update) | async-done | bytes 32784 | tf_op jit(solution)/shard_map/reduce_scatter | solution.py:96
  745.4 1.4 bitcast_convert_fusion.1
  746.8 35.4 %reduce-scatter.6.cloned.1.call-done = bf16[128,512]{1,0:T(8,128)(2,1)} async-done(((bf16[128,4096]{1,0:T(8,128)(2,1)}), bf16[128,512]{1,0:T(8,128)(2,1)}) %reduce-scatter.6.cloned.1.call-update) | async-done | bytes 131088 | tf_op jit(solution)/shard_map/reduce_scatter | solution.py:72
  782.2 36.7 %reduce-scatter.8.cloned.1.call-done = bf16[128,512]{1,0:T(8,128)(2,1)} async-done(((bf16[128,4096]{1,0:T(8,128)(2,1)}), bf16[128,512]{1,0:T(8,128)(2,1)}) %reduce-scatter.8.cloned.1.call-update) | async-done | bytes 131088 | tf_op jit(solution)/shard_map/reduce_scatter | solution.py:101
  (24 shorter events, 0.1 us)
Async XLA Ops:
  7.2 74.2 %copy-start = (bf16[1,32,128,128]{3,2,1,0:T(8,128)(2,1)S(1)}, bf16[1,32,128,128]{3,2,1,0:T(8,128)(2,1)}, u32[]{:S(2)}) copy-start(bf16[1,32,128,128]{3,2,1,0:T(8,128)(2,1)} %param.19) | copy-start | bytes 3145732
  7.2 31.9 %all-gather.3.cloned.1.call-start = ((), (), s32[]{:S(2)}) async-start(), calls=%async_computation.5 | async-start | bytes 1179648 | tf_op jit(solution)/shard_map/all_gather | solution.py:45
  9.0 58.3 %all-gather.5.cloned.1.call-start = ((), (), s32[]{:S(2)}) async-start(), calls=%async_computation.7 | async-start | bytes 1179648 | tf_op jit(solution)/shard_map/all_gather | solution.py:46
  10.7 296.2 %reduce-scatter.10.cloned.1.call-start = ((), (), s32[]{:S(2)}) async-start(), calls=%async_computation.9 | async-start | bytes 1081344 | tf_op jit(solution)/shard_map/reduce_scatter | solution.py:96
  71.2 4.6 copy-start.2
  72.8 3.0 copy-start.8
  76.3 2.3 copy-start.1
  76.3 2.3 copy-start.5
  79.1 2.3 copy-start.6
  90.5 435.7 %reduce-scatter.14.cloned.1.call-start = ((), (), s32[]{:S(2)}) async-start(), calls=%async_computation.11 | async-start | bytes 1081344 | tf_op jit(solution)/shard_map/reduce_scatter | solution.py:96
  95.6 649.8 %reduce-scatter.12.cloned.1.call-start = ((), (), s32[]{:S(2)}) async-start(), calls=%async_computation.10 | async-start | bytes 1081344 | tf_op jit(solution)/shard_map/reduce_scatter | solution.py:96
  97.3 3.4 copy-start.7
  100.6 681.5 %reduce-scatter.6.cloned.1.call-start = ((), (), s32[]{:S(2)}) async-start(), calls=%async_computation.6 | async-start | bytes 1179648 | tf_op jit(solution)/shard_map/reduce_scatter | solution.py:72
  105.6 2.3 copy-start.3
  105.6 713.2 %reduce-scatter.8.cloned.1.call-start = ((), (), s32[]{:S(2)}) async-start(), calls=%async_computation.8 | async-start | bytes 1179648 | tf_op jit(solution)/shard_map/reduce_scatter | solution.py:101
  105.7 2.3 copy-start.4
Sparse Core Ops, SparseCore 0:
  10.4 28.6 all-gather.2
  41.5 25.6 all-gather.4
  90.6 216.3 reduce-scatter.9
  310.6 215.4 reduce-scatter.13
  529.8 215.5 reduce-scatter.11
  748.4 33.7 reduce-scatter.5
  785.3 33.5 reduce-scatter.7
where the time goes:
time: 826 us
  waiting for transfers between devices  749 us (91%)
  matrix products  31 us (4%)
  local copies, waits for them, and re-layouts  21.4 us (3%)
  between operations  14.4 us (2%)
  other arithmetic  9.27 us (1%)
    reduce_scatter x3, waiting for transfers between devices, body(): lax.psum_scatter(term.astype(jnp.bfloat16), 'dp', scatter_dimension=0, ti...  626 us
    reduce_scatter x1, waiting for transfers between devices, body(): lax.psum_scatter(input_part.astype(jnp.bfloat16), 'tensor', scatter_dimen...  36.7 us
    reduce_scatter x1, waiting for transfers between devices, body(): lax.psum_scatter(mixed_part.astype(jnp.bfloat16), 'tensor', scatter_dimen...  35.4 us
    all_gather x1, waiting for transfers between devices, body(): lax.all_gather(grad_out, 'tensor', axis=1, tiled=True)  26.5 us
    all_gather x1, waiting for transfers between devices, body(): lax.all_gather(tokens, 'tensor', axis=1, tiled=True)  24.2 us
  transfers between devices with their start and end apart: 7, of which 7 were waited for; matrix products, arithmetic and copies ran while one was open for 4% of the time, Pallas kernels for 0%

commit v1 on v0

--- a/solution.py
+++ b/solution.py
@@ -4,6 +4,14 @@
 from jax.sharding import PartitionSpec as P
 
 FF = 14336
+
+
+def gather_from_all(shard, axis, dim):
+    size = lax.axis_size(axis)
+    repeats = [size if d == dim else 1 for d in range(shard.ndim)]
+    return lax.all_to_all(
+        jnp.tile(shard, repeats), axis, split_axis=dim, concat_axis=dim, tiled=True
+    )
 
 
 def locate(blocks, feature_count):
@@ -43,7 +51,7 @@
 ):
     gathered_x, gathered_dy = (
         lax.all_gather(tokens, "tensor", axis=1, tiled=True),
-        lax.all_gather(grad_out, "tensor", axis=1, tiled=True),
+        gather_from_all(grad_out, "tensor", 1),
     )
     tok_rows, feature_width = gathered_x.shape
     block_size = gate_values.shape[-1]

time: 826 us -> 794 us (0.961)
  waiting for transfers between devices: 749 us -> 717 us
    all_gather x1 -> x0, waiting for transfers between devices: 26.5 us -> none  [body(): lax.all_gather(grad_out, 'tensor', axis=1, tiled=True)]
    all_gather x1, waiting for transfers between devices: 24.2 us -> 1.47 us  [body(): lax.all_gather(tokens, 'tensor', axis=1, tiled=True)]
    all_to_all x0 -> x1, waiting for transfers between devices: none -> 17.7 us  [gather_from_all(): lax.all_to_all(jnp.tile(shard, repeats), axis, split_axis=dim, concat_axi...]
  transfers between devices with their start and end apart: 7 -> 7, of which waited for: 7 -> 7; matrix products, arithmetic and copies ran while one was open for 4% -> 5% of each run, Pallas kernels for 0% -> 0%
where the time goes in v1:
time: 794 us; the launch traced here: 793 us
  waiting for transfers between devices  717 us (90%)
  matrix products  33.3 us (4%)
  local copies, waits for them, and re-layouts  18.1 us (2%)
  between operations  14.5 us (2%)
    reduce_scatter x3, waiting for transfers between devices, body(): lax.psum_scatter(term.astype(jnp.bfloat16), 'dp', scatter_dimension=0, ti...  626 us
    reduce_scatter x1, waiting for transfers between devices, body(): lax.psum_scatter(input_part.astype(jnp.bfloat16), 'tensor', scatter_dimen...  36.6 us
    reduce_scatter x1, waiting for transfers between devices, body(): lax.psum_scatter(mixed_part.astype(jnp.bfloat16), 'tensor', scatter_dimen...  35.5 us
    all_to_all x1, waiting for transfers between devices, gather_from_all(): lax.all_to_all(jnp.tile(shard, repeats), axis, split_axis=dim, concat_axi...  17.7 us
    dot_general x6, matrix products, spread(): jnp.einsum('tsn,sc->tcn', product, table, precision=lax.Precision.HIGHEST)  16.9 us
  transfers between devices with their start and end apart: 7, of which 7 were waited for; matrix products, arithmetic and copies ran while one was open for 5% of the time, Pallas kernels for 0%

profile of v1, /device:TPU:8, one launch (start us, length us, event | category | flops | bytes accessed | tf_op | source)
XLA Modules:
  0.0 793.3 jit_solution(9133521635743969930)
XLA Ops:
  7.2 0.0 copy-start
  7.2 0.0 copy-start.9
  7.2 0.0 copy-start.10
  7.2 0.0 copy-start.11
  7.2 0.0 all-gather.2.cloned.1.call-start
  7.3 1.7 copy.39
  9.0 0.0 all-gather.2.cloned.1.call-update
  9.0 1.0 copy.47
  10.0 1.1 tile.2
  11.2 4.3 all-to-all-start
  15.5 0.0 reduce-scatter.10.cloned.1.call-start
  15.5 0.0 copy-done.9
  15.6 0.0 copy-done.11
  15.7 17.7 %all-to-all-done = bf16[128,8,512]{0,2,1:T(8,128)(2,1)S(1)} async-done(((bf16[128,8,512]{0,2,1:T(8,128)(2,1)}), bf16[128,8,512]{0,2,1:T(8,128)(2,1)S(1)}, u32[]{:S(2)}, u32[]{:S(2)}) %all-to-all-start) | async-done | bytes 1048608 | tf_op jit(solution)/shard_map/all_to_all | solution.py:12
  33.4 0.7 copy.48
  34.1 0.7 gather_fusion.3
  34.9 0.9 convolution_bitcast_fusion.2
  35.8 0.1 copy-done.6
  35.8 3.2 fusion.4
  39.0 1.5 all-gather.2.cloned.1.call-done
  40.5 1.6 copy.40
  42.1 0.0 copy-start.2
  42.1 1.6 gather_fusion.1
  43.8 1.7 gather_fusion
  45.4 0.0 copy-done.2
  45.4 1.7 convolution_bitcast_fusion.5
  47.2 0.0 copy-start.1
  47.2 2.2 fusion.10
  49.5 0.5 convolution_bitcast_fusion.4
  50.0 2.2 fusion.8
  52.2 1.1 fusion.37
  53.3 1.7 gather_fusion.4
  55.0 3.2 multiply_convert_fusion.2
  58.1 0.0 reduce-scatter.10.cloned.1.call-update
  58.2 0.2 reduce-scatter.14.cloned.1.call-start
  58.4 1.7 gather_fusion.2
  60.1 3.2 multiply_convert_fusion
  63.3 0.0 reduce-scatter.14.cloned.1.call-update
  63.3 0.0 reduce-scatter.12.cloned.1.call-start
  63.4 1.7 gather_fusion.5
  65.0 3.3 multiply_convert_fusion.1
  68.3 0.0 reduce-scatter.12.cloned.1.call-update
  68.4 0.0 reduce-scatter.6.cloned.1.call-start
  68.4 0.5 convolution_bitcast_fusion.3
  68.9 3.0 fusion.14
  71.9 1.4 copy.90
  73.4 0.0 reduce-scatter.6.cloned.1.call-update
  73.4 0.0 copy-start.3
  73.4 0.0 reduce-scatter.8.cloned.1.call-start
  73.4 0.0 copy-start.4
  73.4 2.2 convolution_bitcast_fusion
  75.7 0.9 convolution_bitcast_fusion.1
  76.6 3.0 fusion
  79.6 3.1 add_convert_fusion
  82.8 1.4 copy.89
  84.2 0.0 reduce-scatter.8.cloned.1.call-update
  84.2 190.6 %reduce-scatter.10.cloned.1.call-done = bf16[1,128,128]{2,1,0:T(8,128)(2,1)} async-done(((bf16[32,128,128]{2,1,0:T(8,128)(2,1)}), bf16[1,128,128]{2,1,0:T(8,128)(2,1)}) %reduce-scatter.10.cloned.1.call-update) | async-done | bytes 32784 | tf_op jit(solution)/shard_map/reduce_scatter | solution.py:104
  274.9 1.4 bitcast_convert_fusion.2
  276.2 217.8 %reduce-scatter.14.cloned.1.call-done = bf16[1,128,128]{2,1,0:T(8,128)(2,1)} async-done(((bf16[32,128,128]{2,1,0:T(8,128)(2,1)}), bf16[1,128,128]{2,1,0:T(8,128)(2,1)}) %reduce-scatter.14.cloned.1.call-update) | async-done | bytes 32784 | tf_op jit(solution)/shard_map/reduce_scatter | solution.py:104
  494.0 1.4 bitcast_convert_fusion
  495.4 217.6 %reduce-scatter.12.cloned.1.call-done = bf16[1,128,128]{2,1,0:T(8,128)(2,1)} async-done(((bf16[32,128,128]{2,1,0:T(8,128)(2,1)}), bf16[1,128,128]{2,1,0:T(8,128)(2,1)}) %reduce-scatter.12.cloned.1.call-update) | async-done | bytes 32784 | tf_op jit(solution)/shard_map/reduce_scatter | solution.py:104
  713.0 1.4 bitcast_convert_fusion.1
  714.4 35.5 %reduce-scatter.6.cloned.1.call-done = bf16[128,512]{1,0:T(8,128)(2,1)} async-done(((bf16[128,4096]{1,0:T(8,128)(2,1)}), bf16[128,512]{1,0:T(8,128)(2,1)}) %reduce-scatter.6.cloned.1.call-update) | async-done | bytes 131088 | tf_op jit(solution)/shard_map/reduce_scatter | solution.py:80
  749.9 36.6 %reduce-scatter.8.cloned.1.call-done = bf16[128,512]{1,0:T(8,128)(2,1)} async-done(((bf16[128,4096]{1,0:T(8,128)(2,1)}), bf16[128,512]{1,0:T(8,128)(2,1)}) %reduce-scatter.8.cloned.1.call-update) | async-done | bytes 131088 | tf_op jit(solution)/shard_map/reduce_scatter | solution.py:109
  (30 shorter events, 0.1 us)
Async XLA Ops:
  7.2 27.7 %copy-start = (bf16[1,32,128,128]{3,2,1,0:T(8,128)(2,1)S(1)}, bf16[1,32,128,128]{3,2,1,0:T(8,128)(2,1)}, u32[]{:S(2)}) copy-start(bf16[1,32,128,128]{3,2,1,0:T(8,128)(2,1)} %param.19) | copy-start | bytes 3145732
  7.2 8.3 %copy-start.9 = (s32[1,32]{1,0:T(1,128)S(1)}, s32[1,32]{1,0:T(1,128)}, u32[]{:S(2)}) copy-start(s32[1,32]{1,0:T(1,128)} %param.14) | copy-start | bytes 388
  7.2 8.4 %copy-start.10 = (s32[1,32]{1,0:T(1,128)S(1)}, s32[1,32]{1,0:T(1,128)}, u32[]{:S(2)}) copy-start(s32[1,32]{1,0:T(1,128)} %param.16) | copy-start | bytes 388
  7.2 8.4 %copy-start.11 = (s32[1,32]{1,0:T(1,128)S(1)}, s32[1,32]{1,0:T(1,128)}, u32[]{:S(2)}) copy-start(s32[1,32]{1,0:T(1,128)} %param.18) | copy-start | bytes 388
  7.2 33.3 %all-gather.2.cloned.1.call-start = ((), (), s32[]{:S(2)}) async-start(), calls=%async_computation.6 | async-start | bytes 1179648 | tf_op jit(solution)/shard_map/all_gather | solution.py:53
  11.2 22.3 %all-to-all-start = ((bf16[128,8,512]{0,2,1:T(8,128)(2,1)}), bf16[128,8,512]{0,2,1:T(8,128)(2,1)S(1)}, u32[]{:S(2)}, u32[]{:S(2)}) async-start(bf16[128,8,512]{0,2,1:T(8,128)(2,1)} %tile.2), calls=%async_computation.1 | async-start | bytes 2097152 | tf_op jit(solution)/shard_map/all_to_all | solution.py:12
  15.5 259.4 %reduce-scatter.10.cloned.1.call-start = ((), (), s32[]{:S(2)}) async-start(), calls=%async_computation.9 | async-start | bytes 1081344 | tf_op jit(solution)/shard_map/reduce_scatter | solution.py:104
  34.8 1.0 copy-start.6
  42.1 3.3 copy-start.2
  47.2 2.3 copy-start.1
  47.2 2.3 copy-start.5
  50.0 2.3 copy-start.8
  58.2 435.9 %reduce-scatter.14.cloned.1.call-start = ((), (), s32[]{:S(2)}) async-start(), calls=%async_computation.11 | async-start | bytes 1081344 | tf_op jit(solution)/shard_map/reduce_scatter | solution.py:104
  63.3 649.7 %reduce-scatter.12.cloned.1.call-start = ((), (), s32[]{:S(2)}) async-start(), calls=%async_computation.10 | async-start | bytes 1081344 | tf_op jit(solution)/shard_map/reduce_scatter | solution.py:104
  65.0 3.4 copy-start.7
  68.4 681.5 %reduce-scatter.6.cloned.1.call-start = ((), (), s32[]{:S(2)}) async-start(), calls=%async_computation.7 | async-start | bytes 1179648 | tf_op jit(solution)/shard_map/reduce_scatter | solution.py:80
  73.4 2.3 copy-start.3
  73.4 713.0 %reduce-scatter.8.cloned.1.call-start = ((), (), s32[]{:S(2)}) async-start(), calls=%async_computation.8 | async-start | bytes 1179648 | tf_op jit(solution)/shard_map/reduce_scatter | solution.py:109
  73.4 2.3 copy-start.4
Sparse Core Ops, SparseCore 0:
  10.5 30.0 all-gather.1
  58.3 216.5 reduce-scatter.9
  278.7 215.3 reduce-scatter.13
  497.7 215.2 reduce-scatter.11
  715.9 33.8 reduce-scatter.5
  752.8 33.5 reduce-scatter.7
